TPU v7x, 512 devices: a whole 4x8x8 slice. The times are simulated.
512 devices in a mesh: dp: 4 (over x), shard: 128 (over z, y, core).
Axes of the slice: x: 4, y: 8, z: 8, core: 2. Of those that a mesh axis runs over, the one named last changes fastest.
Arguments:
- grad_parts: float32 [4, 1024, 16384], P('dp', None, 'shard'), may hold values from -0.3 to 0.3
- owner: int32 [1024], replicated, may hold values from 0 to 127, as said below
- master: float32 [4, 128, 4, 128, 128], P('dp', 'shard'), may hold values from -6 to 6
- first_moment: float32 [4, 128, 4, 128, 128], P('dp', 'shard'), may hold values from -0.12 to 0.12
- second_moment: float32 [4, 128, 4, 128, 128], P('dp', 'shard'), may hold values from 0.0001 to 0.001
- left_stat: float32 [4, 128, 4, 128, 128], P('dp', 'shard'), may hold values from -0.0062992126 to 10
- right_stat: float32 [4, 128, 4, 128, 128], P('dp', 'shard'), may hold values from -0.0062992126 to 10
- left_basis: float32 [4, 128, 4, 128, 128], P('dp', 'shard'), may hold values from -0.079549513 to 1.0795495
- right_basis: float32 [4, 128, 4, 128, 128], P('dp', 'shard'), may hold values from -0.079549513 to 1.0795495
Outputs:
- new_params: bfloat16 [1024, 16384], P(None, 'shard')
- master_out: float32 [4, 128, 4, 128, 128], P('dp', 'shard')
- first_out: float32 [4, 128, 4, 128, 128], P('dp', 'shard')
- second_out: float32 [4, 128, 4, 128, 128], P('dp', 'shard')
- left_stat_out: float32 [4, 128, 4, 128, 128], P('dp', 'shard')
- right_stat_out: float32 [4, 128, 4, 128, 128], P('dp', 'shard')
- left_basis_out: float32 [4, 128, 4, 128, 128], P('dp', 'shard')
- right_basis_out: float32 [4, 128, 4, 128, 128], P('dp', 'shard')
Inputs may be any that keep to these rules, and one draw needn't show every extreme that they name: In each group of 256 consecutive tiles no owner index holds more than 4 tiles, and some owner holds exactly 4.
All inputs are finite; a program needn't handle non-finite values.
Results may differ from a plain program's by a relative error of at most 0.001.
Values may be sent and summed in bfloat16 or wider, within the bound.
No kernel may reach another device: no remote copies, remote signals or barrier semaphores. Data moves between devices by JAX's collectives and lax.ppermute only.
A program may use at most 64 MiB of HBM per device.

v0:
```python
import jax
import jax.numpy as jnp
from jax import lax
from jax.sharding import PartitionSpec as P

NS_STEPS = 10
beta_one = 0.9
beta_two = 0.95
stat_decay = 0.95
learn_rate = 0.05
weight_decay = 0.01
adam_eps = 1e-08
highest = lax.Precision.HIGHEST


def product(form, left, right):
    return jnp.einsum(form, left, right, precision=highest)


def slot_index(owners, shards):
    matches = (owners[..., None] == jnp.arange(shards, dtype=jnp.int32)).astype(jnp.int32)
    running = jnp.cumsum(matches, axis=1)
    return jnp.sum(matches * running, axis=-1) - 1


def orthogonal(pending):
    iterate = pending * lax.rsqrt(jnp.sum(pending * pending, axis=(1, 2), keepdims=True) + 1e-06)
    for step in range(NS_STEPS):
        gram = product("nik,njk->nij", iterate, iterate)
        iterate = 1.5 * iterate - 0.5 * product("nij,njk->nik", gram, iterate)
    return iterate


def soap_update(gradient, master, first, second, lstat, rstat, lbasis, rbasis):
    first_new = beta_one * first + (1.0 - beta_one) * gradient
    grad_rot = product("nik,nkl->nil", product("nji,njk->nik", lbasis, gradient), rbasis)
    first_rot = product("nik,nkl->nil", product("nji,njk->nik", lbasis, first_new), rbasis)
    second_new = beta_two * second + (1.0 - beta_two) * grad_rot * grad_rot
    normed = first_rot / (jnp.sqrt(second_new) + adam_eps)
    update = product("nik,nlk->nil", product("nij,njk->nik", lbasis, normed), rbasis)
    master_new = master - learn_rate * (update + weight_decay * master)
    lstat_new = stat_decay * lstat + (1.0 - stat_decay) * product(
        "nik,njk->nij", gradient, gradient
    )
    rstat_new = stat_decay * rstat + (1.0 - stat_decay) * product(
        "nki,nkj->nij", gradient, gradient
    )
    lbasis_new = orthogonal(product("nij,njk->nik", lstat_new, lbasis))
    rbasis_new = orthogonal(product("nij,njk->nik", rstat_new, rbasis))
    return (master_new, first_new, second_new, lstat_new, rstat_new, lbasis_new, rbasis_new)


def body(
    grad_parts,
    owner,
    master,
    first_moment,
    second_moment,
    left_stat,
    right_stat,
    left_basis,
    right_basis,
):
    shards = lax.axis_size("shard")
    groups = lax.axis_size("dp")
    my_group = lax.axis_index("dp")
    capacity = master.shape[2]
    block_size = master.shape[4]
    piece_len = grad_parts.shape[2]
    tile_count = owner.shape[0]
    per_group = tile_count // groups
    owners = owner.reshape(groups, per_group)
    place_index = slot_index(owners, shards) * shards + owners
    own_place = lax.dynamic_index_in_dim(place_index, my_group, 0, keepdims=False)
    summed = lax.psum_scatter(grad_parts, "dp", scatter_dimension=1, tiled=True)
    outgoing = jnp.zeros((capacity * shards, piece_len), jnp.float32)
    outgoing = outgoing.at[own_place].set(summed[0])
    outgoing = outgoing.reshape(capacity, shards, piece_len)
    incoming = lax.all_to_all(outgoing, "shard", split_axis=1, concat_axis=1, tiled=True)

    def as_tiles(array):
        return array.reshape(capacity, block_size, block_size)

    results = soap_update(
        incoming,
        as_tiles(master),
        as_tiles(first_moment),
        as_tiles(second_moment),
        as_tiles(left_stat),
        as_tiles(right_stat),
        as_tiles(left_basis),
        as_tiles(right_basis),
    )
    shaped = [item.reshape(1, 1, capacity, block_size, block_size) for item in results]
    weights = results[0].astype(jnp.bfloat16)
    returned = lax.all_to_all(weights, "shard", split_axis=1, concat_axis=1, tiled=True)
    returned = returned.reshape(capacity * shards, piece_len)
    own_rows = returned[own_place]
    new_params = lax.all_gather(own_rows, "dp", axis=0, tiled=True)
    return (new_params, shaped[0], shaped[1], shaped[2], shaped[3], shaped[4], shaped[5], shaped[6])


def solution(mesh):
    placed = (
        P("dp", None, "shard"),
        P(),
        P("dp", "shard", None, None, None),
        P("dp", "shard", None, None, None),
        P("dp", "shard", None, None, None),
        P("dp", "shard", None, None, None),
        P("dp", "shard", None, None, None),
        P("dp", "shard", None, None, None),
        P("dp", "shard", None, None, None),
    )
    return jax.shard_map(
        body,
        mesh=mesh,
        in_specs=placed,
        out_specs=(
            P(None, "shard"),
            P("dp", "shard", None, None, None),
            P("dp", "shard", None, None, None),
            P("dp", "shard", None, None, None),
            P("dp", "shard", None, None, None),
            P("dp", "shard", None, None, None),
            P("dp", "shard", None, None, None),
            P("dp", "shard", None, None, None),
        ),
        check_vma=False,
    )
```

profile of v0, /device:TPU:8, one launch (start us, length us, event | category | flops | bytes accessed | tf_op | source)
XLA Modules:
  0.0 143.0 jit_solution(8679170944378737934)
XLA Ops:
  7.2 0.7 reduce-scatter.2.cloned.1.call-update
  7.9 0.7 copy-done.10
  8.8 0.9 fusion.26
  10.3 31.9 %reduce-scatter.2.cloned.1.call-done = f32[1,256,128]{2,1,0:T(8,128)} async-done(((f32[1,1024,128]{2,1,0:T(8,128)}), f32[1,256,128]{2,1,0:T(8,128)}) %reduce-scatter.2.cloned.1.call-update) | async-done | bytes 131088 | tf_op jit(solution)/shard_map/reduce_scatter | solution.py:75
  42.2 1.6 %scatter_custom_fusion = f32[512,128]{1,0:T(8,128)S(1)} fusion(s32[256]{0:T(256)S(1)} %bitcast.159, f32[1,256,128]{2,1,0:T(8,128)} %reduce-scatter.2.cloned.1.call-done, f32[]{:T(128)} %constant.18.clone.1), kind=kCustom, calls=%fused_computation.91 | custom fusion | bytes 393220 | tf_op jit(solution)/shard_map/scatter | solution.py:77
  43.8 0.9 copy.40
  44.7 14.5 %all-to-all-start = ((f32[4,128,128]{2,0,1:T(4,128)}), f32[4,128,128]{2,0,1:T(4,128)S(1)}, u32[]{:S(2)}, u32[]{:S(2)}) async-start(f32[4,128,128]{2,0,1:T(4,128)} %copy.40), calls=%async_computation.1 | async-start | bytes 524288 | tf_op jit(solution)/shard_map/all_to_all | solution.py:79
  59.2 14.5 %all-to-all-done = f32[4,128,128]{2,0,1:T(4,128)S(1)} async-done(((f32[4,128,128]{2,0,1:T(4,128)}), f32[4,128,128]{2,0,1:T(4,128)S(1)}, u32[]{:S(2)}, u32[]{:S(2)}) %all-to-all-start) | async-done | bytes 262176 | tf_op jit(solution)/shard_map/all_to_all | solution.py:79
  74.9 0.8 fusion.51
  77.2 0.7 fusion.77
  78.3 0.7 fusion.78
  81.5 0.7 fusion.81
  88.0 0.8 fusion.54
  90.3 0.8 fusion.68
  102.0 1.4 fusion.66
  103.4 0.8 copy.47
  104.1 6.1 %all-to-all-start.1 = ((bf16[4,128,128]{2,0,1:T(4,128)(2,1)}), bf16[4,128,128]{2,0,1:T(4,128)(2,1)S(1)}, u32[]{:S(2)}, u32[]{:S(2)}) async-start(bf16[4,128,128]{2,0,1:T(4,128)(2,1)} %copy.47), calls=%async_computation.2 | async-start | bytes 262144 | tf_op jit(solution)/shard_map/all_to_all | solution.py:96
  110.2 0.7 copy.53
  111.0 1.1 fusion.1
  112.1 1.1 fusion.12
  113.2 9.1 %all-to-all-done.1 = bf16[4,128,128]{2,0,1:T(4,128)(2,1)S(1)} async-done(((bf16[4,128,128]{2,0,1:T(4,128)(2,1)}), bf16[4,128,128]{2,0,1:T(4,128)(2,1)S(1)}, u32[]{:S(2)}, u32[]{:S(2)}) %all-to-all-start.1) | async-done | bytes 131104 | tf_op jit(solution)/shard_map/all_to_all | solution.py:96
  122.3 0.9 gather_fusion
  123.2 12.3 %all-gather = bf16[1024,128]{1,0:T(8,128)(2,1)S(1)} all-gather(bf16[256,128]{1,0:T(8,128)(2,1)S(1)} %gather_fusion), channel_id=2, replica_groups=mesh['dp'=4,'shard'=128] {'dp'}, dimensions={0}, use_global_device_ids=true | all-gather | bytes 327680 | tf_op jit(solution)/shard_map/all_gather | solution.py:99
  135.5 0.7 copy.69
  (79 shorter events, 24.6 us)
Async XLA Ops:
  7.2 67.0 %copy-start = (f32[1,1,4,128,128]{4,3,2,1,0:T(8,128)S(1)}, f32[1,1,4,128,128]{4,3,2,1,0:T(8,128)}, u32[]{:S(2)}) copy-start(f32[1,1,4,128,128]{4,3,2,1,0:T(8,128)} %param.17) | copy-start | bytes 786436
  7.2 35.0 %reduce-scatter.2.cloned.1.call-start = ((), (), s32[]{:S(2)}) async-start(), calls=%async_computation.3 | async-start | bytes 655360 | tf_op jit(solution)/shard_map/reduce_scatter | solution.py:75
  7.9 0.7 copy-start.10
  44.6 14.5 %copy-start.6 = (f32[1,1,4,128,128]{4,3,2,1,0:T(8,128)S(1)}, f32[1,1,4,128,128]{4,3,2,1,0:T(8,128)}, u32[]{:S(2)}) copy-start(f32[1,1,4,128,128]{4,3,2,1,0:T(8,128)} %param.12) | copy-start | bytes 786436
  44.7 29.0 %all-to-all-start = ((f32[4,128,128]{2,0,1:T(4,128)}), f32[4,128,128]{2,0,1:T(4,128)S(1)}, u32[]{:S(2)}, u32[]{:S(2)}) async-start(f32[4,128,128]{2,0,1:T(4,128)} %copy.40), calls=%async_computation.1 | async-start | bytes 524288 | tf_op jit(solution)/shard_map/all_to_all | solution.py:79
  59.2 14.6 %copy-start.7 = (f32[1,1,4,128,128]{4,3,2,1,0:T(8,128)S(1)}, f32[1,1,4,128,128]{4,3,2,1,0:T(8,128)}, u32[]{:S(2)}) copy-start(f32[1,1,4,128,128]{4,3,2,1,0:T(8,128)} %param.15) | copy-start | bytes 786436
  74.2 0.7 copy-start.3
  84.8 1.0 copy-start.1
  85.7 0.9 copy-start.5
  87.3 0.7 copy-start.2
  99.0 1.0 copy-start.8
  100.3 0.7 copy-start.4
  101.1 0.9 copy-start.9
  104.1 18.2 %all-to-all-start.1 = ((bf16[4,128,128]{2,0,1:T(4,128)(2,1)}), bf16[4,128,128]{2,0,1:T(4,128)(2,1)S(1)}, u32[]{:S(2)}, u32[]{:S(2)}) async-start(bf16[4,128,128]{2,0,1:T(4,128)(2,1)} %copy.47), calls=%async_computation.2 | async-start | bytes 262144 | tf_op jit(solution)/shard_map/all_to_all | solution.py:96
Sparse Core Ops, SparseCore 0:
  10.8 31.2 reduce-scatter.1
where the time goes:
time: 143 us
  waiting for transfers between devices  56.1 us (39%)
  matrix products  28.9 us (20%)
  starting transfers between devices  20.6 us (14%)
  between operations  14.6 us (10%)
  blocking collectives  12.3 us (9%)
  local copies, waits for them, and re-layouts  8.78 us (6%)
  other arithmetic  1.75 us (1%)
    reduce_scatter x1, waiting for transfers between devices, body(): summed = lax.psum_scatter(grad_parts, 'dp', scatter_dimension=1, tiled=True)  31.9 us
    dot_general x50, matrix products, product(): return jnp.einsum(form, left, right, precision=highest)  28.9 us
    all_to_all x1, waiting for transfers between devices, body(): lax.all_to_all(outgoing, 'shard', split_axis=1, concat_axis=1, tiled=True)  14.5 us
    all_to_all x1, starting transfers between devices, body(): lax.all_to_all(outgoing, 'shard', split_axis=1, concat_axis=1, tiled=True)  14.5 us
    all_gather x1, blocking collectives, body(): new_params = lax.all_gather(own_rows, 'dp', axis=0, tiled=True)  12.3 us
    all_to_all x1, waiting for transfers between devices, body(): lax.all_to_all(weights, 'shard', split_axis=1, concat_axis=1, tiled=True)  9.13 us
    all_to_all x1, starting transfers between devices, body(): lax.all_to_all(weights, 'shard', split_axis=1, concat_axis=1, tiled=True)  6.1 us
    unnamed x24, local copies, waits for them, and re-layouts  4.36 us
  transfers between devices with their start and end apart: 3, of which 3 were waited for; matrix products, arithmetic and copies ran while one was open for 3% of the time, Pallas kernels for 0%

commit v1 on v0

--- a/solution.py
+++ b/solution.py
@@ -76,7 +76,12 @@
     outgoing = jnp.zeros((capacity * shards, piece_len), jnp.float32)
     outgoing = outgoing.at[own_place].set(summed[0])
     outgoing = outgoing.reshape(capacity, shards, piece_len)
-    incoming = lax.all_to_all(outgoing, "shard", split_axis=1, concat_axis=1, tiled=True)
+    incoming = jnp.concatenate(
+        lax.all_to_all(
+            jnp.stack(jnp.split(outgoing, lax.axis_size("shard"), axis=1)), "shard", 0, 0
+        ),
+        axis=1,
+    )
 
     def as_tiles(array):
         return array.reshape(capacity, block_size, block_size)

time: 143 us -> 217 us (1.52)
  local copies, waits for them, and re-layouts: 8.78 us -> 82.9 us
    unnamed x24 -> x152, local copies, waits for them, and re-layouts: 4.36 us -> 78.5 us
  transfers between devices with their start and end apart: 3 -> 3, of which waited for: 3 -> 3; matrix products, arithmetic and copies ran while one was open for 3% -> 2% of each run, Pallas kernels for 0% -> 0%
where the time goes in v1:
time: 217 us
  local copies, waits for them, and re-layouts  82.9 us (38%)
  waiting for transfers between devices  55.9 us (26%)
  matrix products  29.1 us (13%)
  starting transfers between devices  20.6 us (9%)
  between operations  14.7 us (7%)
  blocking collectives  12.3 us (6%)
    unnamed x152, local copies, waits for them, and re-layouts  78.5 us
    reduce_scatter x1, waiting for transfers between devices, body(): summed = lax.psum_scatter(grad_parts, 'dp', scatter_dimension=1, tiled=True)  31.9 us
    dot_general x50, matrix products, product(): return jnp.einsum(form, left, right, precision=highest)  29.1 us
    all_to_all x1, starting transfers between devices, body(): lax.all_to_all(jnp.stack(jnp.split(outgoing, lax.axis_size('shard'), axis...  14.5 us
    all_to_all x1, waiting for transfers between devices, body(): lax.all_to_all(jnp.stack(jnp.split(outgoing, lax.axis_size('shard'), axis...  14.4 us
    all_gather x1, blocking collectives, body(): new_params = lax.all_gather(own_rows, 'dp', axis=0, tiled=True)  12.3 us
    all_to_all x1, waiting for transfers between devices, body(): lax.all_to_all(weights, 'shard', split_axis=1, concat_axis=1, tiled=True)  9.02 us
    all_to_all x1, starting transfers between devices, body(): lax.all_to_all(weights, 'shard', split_axis=1, concat_axis=1, tiled=True)  6.1 us
  transfers between devices with their start and end apart: 3, of which 3 were waited for; matrix products, arithmetic and copies ran while one was open for 2% of the time, Pallas kernels for 0%

profile of v1, /device:TPU:8, one launch (start us, length us, event | category | flops | bytes accessed | tf_op | source)
XLA Modules:
  0.0 217.0 jit_solution(11143990003572073373)
XLA Ops:
  7.2 0.7 reduce-scatter.2.cloned.1.call-update
  7.9 0.7 copy-done.10
  8.8 0.9 fusion.26
  10.3 31.9 %reduce-scatter.2.cloned.1.call-done = f32[1,256,128]{2,1,0:T(8,128)} async-done(((f32[1,1024,128]{2,1,0:T(8,128)}), f32[1,256,128]{2,1,0:T(8,128)}) %reduce-scatter.2.cloned.1.call-update) | async-done | bytes 131088 | tf_op jit(solution)/shard_map/reduce_scatter | solution.py:75
  42.2 1.6 scatter_custom_fusion
  118.2 14.5 %all-to-all-start = ((f32[128,4,1,128]{3,1,2,0:T(4,128)}), f32[128,4,1,128]{3,1,2,0:T(4,128)S(1)}, u32[]{:S(2)}, u32[]{:S(2)}) async-start(f32[128,4,1,128]{3,1,2,0:T(4,128)} %constant_dynamic-update-slice_fusion), calls=%async_computation.1 | async-start | bytes 524288 | tf_op jit(solution)/shard_map/all_to_all | solution.py:80
  132.8 14.4 %all-to-all-done = f32[128,4,1,128]{3,1,2,0:T(4,128)S(1)} async-done(((f32[128,4,1,128]{3,1,2,0:T(4,128)}), f32[128,4,1,128]{3,1,2,0:T(4,128)S(1)}, u32[]{:S(2)}, u32[]{:S(2)}) %all-to-all-start) | async-done | bytes 262176 | tf_op jit(solution)/shard_map/all_to_all | solution.py:80
  148.5 0.9 copy-done.5
  149.4 0.7 fusion.22
  150.8 0.8 fusion.53
  152.0 0.7 fusion.90
  154.2 0.7 fusion.92
  162.9 0.8 fusion.56
  164.1 0.9 fusion.81
  176.0 1.4 fusion.80
  177.4 0.8 copy.411
  178.1 6.1 %all-to-all-start.1 = ((bf16[4,128,128]{2,0,1:T(4,128)(2,1)}), bf16[4,128,128]{2,0,1:T(4,128)(2,1)S(1)}, u32[]{:S(2)}, u32[]{:S(2)}) async-start(bf16[4,128,128]{2,0,1:T(4,128)(2,1)} %copy.411), calls=%async_computation.2 | async-start | bytes 262144 | tf_op jit(solution)/shard_map/all_to_all | solution.py:101
  184.2 0.8 copy.416
  185.1 1.1 fusion.1
  186.2 1.1 fusion.12
  187.3 9.0 %all-to-all-done.1 = bf16[4,128,128]{2,0,1:T(4,128)(2,1)S(1)} async-done(((bf16[4,128,128]{2,0,1:T(4,128)(2,1)}), bf16[4,128,128]{2,0,1:T(4,128)(2,1)S(1)}, u32[]{:S(2)}, u32[]{:S(2)}) %all-to-all-start.1) | async-done | bytes 131104 | tf_op jit(solution)/shard_map/all_to_all | solution.py:101
  196.3 0.9 gather_fusion
  197.2 12.3 %all-gather = bf16[1024,128]{1,0:T(8,128)(2,1)S(1)} all-gather(bf16[256,128]{1,0:T(8,128)(2,1)S(1)} %gather_fusion), channel_id=2, replica_groups=mesh['dp'=4,'shard'=128] {'dp'}, dimensions={0}, use_global_device_ids=true | all-gather | bytes 327680 | tf_op jit(solution)/shard_map/all_gather | solution.py:104
  209.5 0.7 copy.685
  (213 shorter events, 98.5 us)
Async XLA Ops:
  7.2 142.9 %copy-start = (f32[1,1,4,128,128]{4,3,2,1,0:T(8,128)S(1)}, f32[1,1,4,128,128]{4,3,2,1,0:T(8,128)}, u32[]{:S(2)}) copy-start(f32[1,1,4,128,128]{4,3,2,1,0:T(8,128)} %param.17) | copy-start | bytes 786436
  7.2 35.0 %reduce-scatter.2.cloned.1.call-start = ((), (), s32[]{:S(2)}) async-start(), calls=%async_computation.3 | async-start | bytes 655360 | tf_op jit(solution)/shard_map/reduce_scatter | solution.py:75
  7.9 0.7 copy-start.10
  118.2 14.5 %copy-start.7 = (f32[1,1,4,128,128]{4,3,2,1,0:T(8,128)S(1)}, f32[1,1,4,128,128]{4,3,2,1,0:T(8,128)}, u32[]{:S(2)}) copy-start(f32[1,1,4,128,128]{4,3,2,1,0:T(8,128)} %param.12) | copy-start | bytes 786436
  118.2 29.0 %all-to-all-start = ((f32[128,4,1,128]{3,1,2,0:T(4,128)}), f32[128,4,1,128]{3,1,2,0:T(4,128)S(1)}, u32[]{:S(2)}, u32[]{:S(2)}) async-start(f32[128,4,1,128]{3,1,2,0:T(4,128)} %constant_dynamic-update-slice_fusion), calls=%async_computation.1 | async-start | bytes 524288 | tf_op jit(solution)/shard_map/all_to_all | solution.py:80
  132.8 14.5 %copy-start.1 = (f32[1,1,4,128,128]{4,3,2,1,0:T(8,128)S(1)}, f32[1,1,4,128,128]{4,3,2,1,0:T(8,128)}, u32[]{:S(2)}) copy-start(f32[1,1,4,128,128]{4,3,2,1,0:T(8,128)} %param.16) | copy-start | bytes 786436
  148.5 1.0 copy-start.5
  150.1 0.7 copy-start.2
  160.7 1.0 copy-start.6
  162.2 0.7 copy-start.3
  172.9 1.0 copy-start.8
  174.3 0.7 copy-start.4
  175.0 0.9 copy-start.9
  178.1 18.2 %all-to-all-start.1 = ((bf16[4,128,128]{2,0,1:T(4,128)(2,1)}), bf16[4,128,128]{2,0,1:T(4,128)(2,1)S(1)}, u32[]{:S(2)}, u32[]{:S(2)}) async-start(bf16[4,128,128]{2,0,1:T(4,128)(2,1)} %copy.411), calls=%async_computation.2 | async-start | bytes 262144 | tf_op jit(solution)/shard_map/all_to_all | solution.py:101
Sparse Core Ops, SparseCore 0:
  10.8 31.2 reduce-scatter.1
